TPU v7x, 32 devices: a whole 2x2x4 slice. The times are simulated.
32 devices in a mesh: parts: 2 (over y), req: 8 (over z, x), mp: 2 (over core).
Axes of the slice: x: 2, y: 2, z: 4, core: 2. Of those that a mesh axis runs over, the one named last changes fastest.
Arguments:
- hidden: bfloat16 [2048, 8192], P(('parts', 'req'), 'mp'), parts along dimension 0, may hold values from -6 to 6
- base_query_block: bfloat16 [2048, 1024], P(('parts', 'req'), 'mp'), parts along dimension 0, may hold values from -112 to 112
- key_value_block: bfloat16 [2048, 256], P(('parts', 'req')), parts along dimension 0, may hold values from -7.1875 to 7.1875
- prefix_page_store: bfloat16 [256, 32, 256], P(('parts', 'req')), parts along dimension 0, may hold values from -8 to 8
- adapter_down_weight: bfloat16 [8, 2, 64, 4096], P('req', 'mp'), may hold values from -0.0625 to 0.0625
- adapter_up_weight: bfloat16 [8, 2, 64, 512], P('req', 'mp'), may hold values from -0.75 to 0.75
- request_adapter: int32 [16], P(('parts', 'req')), parts along dimension 0, may hold values from 0 to 7
- prefix_page_count: int32 [16], P(('parts', 'req')), parts along dimension 0, may hold values from 2 to 8, as said below
- page_owner_groups: int32 [16, 8], P(('parts', 'req')), parts along dimension 0, may hold values from 0 to 7, as said below
- page_pool_row: int32 [16, 8], P(('parts', 'req')), parts along dimension 0, may hold values from 0 to 15
Outputs:
- attn_out: bfloat16 [2048, 1024], P(('parts', 'req'), 'mp'), parts along dimension 0
There are 2 independent parts, one for each index of `parts`. A program takes and returns all parts, laid end to end along the dimension named above; an argument that names none is the same for every part. Nothing has to cross between parts.
Inputs may be any that keep to these rules, and one draw needn't show every extreme that they name: `prefix_page_count`: some request has exactly 8 prefix pages. `page_owner_groups`: each row names every request group once; its first prefix_page_count[r] entries hold request r's prefix pages, the rest is padding.
All inputs are finite; a program needn't handle non-finite values.
Results may differ from a plain program's by a relative error of at most 0.025.
Values may be sent and summed in bfloat16 or wider, within the bound.
No kernel may reach another device: no remote copies, remote signals or barrier semaphores. Data moves between devices by JAX's collectives and lax.ppermute only.
A program may use at most 64 MiB of HBM per device.

v0:
```python
import math
import jax
import jax.numpy as jnp
from jax import lax
from jax.sharding import PartitionSpec as P

ROPE_BASE = 500000.0
LANES = 128
TILE_ROWS = 16


def rotate(vectors, positions):
    head_width = vectors.shape[-1]
    half_dim = head_width // 2
    frequency = ROPE_BASE ** (-2.0 * jnp.arange(half_dim, dtype=jnp.float32) / head_width)
    angles = positions.astype(jnp.float32)[:, None] * frequency[None, :]
    cosine = jnp.concatenate([jnp.cos(angles), jnp.cos(angles)], axis=1)[:, None, :]
    sine_part = jnp.concatenate([jnp.sin(angles), jnp.sin(angles)], axis=1)[:, None, :]
    turned = jnp.concatenate([-vectors[..., half_dim:], vectors[..., :half_dim]], axis=-1)
    return vectors * cosine + turned * sine_part


def tiled_ok(shape, groups):
    rows, cols = shape
    if rows % TILE_ROWS or cols % LANES:
        return False
    return rows // TILE_ROWS * (cols // LANES) % groups == 0


def to_pieces(matrix, groups):
    rows, cols = matrix.shape
    if tiled_ok(matrix.shape, groups):
        tiles = matrix.reshape(rows // TILE_ROWS, TILE_ROWS, cols // LANES, LANES)
        tiles = jnp.transpose(tiles, (0, 2, 1, 3))
        return tiles.reshape(groups, -1, LANES)
    flat = matrix.reshape(groups, -1)
    extra = -flat.shape[1] % LANES
    if extra:
        flat = jnp.pad(flat, ((0, 0), (0, extra)))
    return flat.reshape(groups, -1, LANES)


def from_pieces(pieces, shape):
    rows, cols = shape
    groups = pieces.shape[0]
    if tiled_ok(shape, groups):
        tiles = pieces.reshape(rows // TILE_ROWS, cols // LANES, TILE_ROWS, LANES)
        tiles = jnp.transpose(tiles, (0, 2, 1, 3))
        return tiles.reshape(rows, cols)
    flat = pieces.reshape(groups, -1)[:, : rows * cols // groups]
    return flat.reshape(rows, cols)


def piece_rows(shape, groups):
    rows, cols = shape
    if tiled_ok(shape, groups):
        return rows * cols // groups // LANES
    return -(-(rows * cols // groups) // LANES)


def attend(queries, all_keys, all_values, allowed):
    token_count, head_count, head_width = queries.shape
    score_scale = 1.0 / math.sqrt(head_width)
    rows = queries.reshape(token_count * head_count, head_width)
    scores = (
        lax.dot_general(
            rows, all_keys, (((1,), (1,)), ((), ())), preferred_element_type=jnp.float32
        )
        * score_scale
    )
    scores = scores.reshape(token_count, head_count, -1)
    scores = jnp.where(allowed[:, None, :], scores, -jnp.inf)
    row_max = jnp.max(scores, axis=2, keepdims=True)
    weights = jnp.exp(scores - row_max)
    weights_bf = (weights / jnp.sum(weights, axis=2, keepdims=True)).astype(jnp.bfloat16)
    out = jnp.dot(
        weights_bf.reshape(token_count * head_count, -1),
        all_values,
        preferred_element_type=jnp.float32,
    ).astype(jnp.bfloat16)
    return out.reshape(token_count, head_count * head_width)


def on_device(
    hidden,
    base_query_block,
    key_value_block,
    prefix_page_store,
    adapter_down_weight,
    adapter_up_weight,
    request_adapter,
    prefix_page_count,
    page_owner_groups,
    page_pool_row,
):
    groups = lax.axis_size("req")
    head_width = key_value_block.shape[1] // 2
    total_row_count = hidden.shape[0]
    page_len = prefix_page_store.shape[1]
    held = adapter_down_weight.shape[0]
    down_shape = adapter_down_weight.shape[2:]
    up_shape = adapter_up_weight.shape[2:]
    down_rows = piece_rows(down_shape, groups)
    up_rows = piece_rows(up_shape, groups)
    page_count = prefix_page_count[0]
    slot_order = jnp.arange(page_owner_groups.shape[1], dtype=jnp.int32)
    live_slots = slot_order < page_count
    holder_order = jnp.arange(groups, dtype=jnp.int32)
    matched = (page_owner_groups[0][None, :] == holder_order[:, None]) & live_slots[None, :]
    wanted = jnp.max(jnp.where(matched, page_pool_row[0][None, :], -1), axis=1)
    asks = jnp.zeros((groups, 1, LANES), jnp.float32)
    asks = asks.at[:, 0, 0].set(jnp.maximum(wanted, 0).astype(jnp.float32))
    asks = asks.at[:, 0, 1].set(request_adapter[0].astype(jnp.float32))
    parts_out = []
    for a in range(held):
        parts_out.append(to_pieces(adapter_down_weight[a, 0], groups))
        parts_out.append(to_pieces(adapter_up_weight[a, 0], groups))
    parts_out.append(asks.astype(jnp.bfloat16))
    stage_one = jnp.concatenate(parts_out, axis=1)
    stage_one = lax.all_to_all(stage_one, "req", split_axis=0, concat_axis=0, tiled=True)
    share_rows = down_rows + up_rows
    shares = stage_one[:, : held * share_rows].reshape(groups * held, share_rows, LANES)
    their_asks = stage_one[:, held * share_rows, :2].astype(jnp.int32)
    their_pages = their_asks[:, 0]
    their_adapters = their_asks[:, 1]
    picked = jnp.take(shares, their_adapters, axis=0)
    pages = jnp.take(prefix_page_store, their_pages, axis=0)
    page_pieces = jax.vmap(lambda page: to_pieces(page, 1)[0])(pages)
    stage_two = jnp.concatenate([picked, page_pieces], axis=1)
    stage_two = lax.all_to_all(stage_two, "req", split_axis=0, concat_axis=0, tiled=True)
    down_projected_rows = from_pieces(stage_two[:, :down_rows], down_shape)
    up_projected_rows = from_pieces(stage_two[:, down_rows:share_rows], up_shape)
    fetched = jax.vmap(lambda piece: from_pieces(piece[None], (page_len, 2 * head_width)))(
        stage_two[:, share_rows:]
    )
    partial_value = lax.dot_general(
        hidden, down_projected_rows, (((1,), (1,)), ((), ())), preferred_element_type=jnp.float32
    )
    rank_reduce = lax.psum(partial_value, "mp").astype(jnp.bfloat16)
    adapter_delta = jnp.dot(rank_reduce, up_projected_rows, preferred_element_type=jnp.float32)
    query_head_count = base_query_block.shape[1] // head_width
    positions = page_len * page_count + jnp.arange(total_row_count, dtype=jnp.int32)
    reduced_sum = (base_query_block.astype(jnp.float32) + adapter_delta).reshape(
        total_row_count, query_head_count, head_width
    )
    queries = rotate(reduced_sum, positions).astype(jnp.bfloat16)
    block_keys = rotate(key_value_block[:, None, :head_width].astype(jnp.float32), positions)[
        :, 0
    ].astype(jnp.bfloat16)
    flat_pages = fetched.reshape(groups * page_len, 2 * head_width)
    prefix_mask = jnp.repeat(wanted >= 0, page_len)
    all_keys = jnp.concatenate([flat_pages[:, :head_width], block_keys], axis=0)
    all_values = jnp.concatenate(
        [flat_pages[:, head_width:], key_value_block[:, head_width:]], axis=0
    )
    token_order = jnp.arange(total_row_count, dtype=jnp.int32)
    causal = token_order[:, None] >= token_order[None, :]
    allowed = jnp.concatenate(
        [jnp.broadcast_to(prefix_mask[None, :], (total_row_count, groups * page_len)), causal],
        axis=1,
    )
    return attend(queries, all_keys, all_values, allowed)


def solution(mesh):
    in_specs = (
        P(("parts", "req"), "mp"),
        P(("parts", "req"), "mp"),
        P(("parts", "req"), None),
        P(("parts", "req"), None, None),
        P("req", "mp", None, None),
        P("req", "mp", None, None),
        P(("parts", "req")),
        P(("parts", "req")),
        P(("parts", "req"), None),
        P(("parts", "req"), None),
    )
    out_specs = P(("parts", "req"), "mp")
    return jax.shard_map(
        on_device, mesh=mesh, in_specs=in_specs, out_specs=out_specs, check_vma=False
    )
```

profile of v0, /device:TPU:0, one launch (start us, length us, event | category | flops | bytes accessed | tf_op | source)
XLA Modules:
  0.0 64.4 jit_solution(6399788822573083362)
XLA Ops:
  0.8 0.8 %select_reduce_fusion = s32[8]{0:T(128)S(1)} fusion(s32[8]{0:T(128)} %bitcast.92, s32[8]{0:T(128)} %bitcast.93, pred[8]{0:T(512)(128)(4,1)S(1)} %iota_compare_fusion.2), kind=kLoop, calls=%fused_computation.48 | loop fusion | flops 248 | bytes 104 | tf_op jit(solution)/shard_map/reduce_max | solution.py:110
  2.3 0.7 %slice.88 = s32[1]{0:T(128)} slice(s32[2]{0:T(128)S(1)} %iota.33), slice={[1:2]} | slice | bytes 8 | tf_op jit(solution)/shard_map/slice.52
  3.0 1.1 %copy.90 = bf16[8,8,32,128]{3,2,1,0:T(8,128)(2,1)S(1)} copy(bf16[8,8,32,128]{3,1,2,0:T(8,128)(2,1)} %bitcast.84) | data formatting | bytes 1048576
  4.2 0.2 copy.76
  4.4 0.6 copy-done.4
  5.0 1.3 %scatter.9 = bf16[8,1,128]{2,1,0:T(2,128)(2,1)S(1)} dynamic-update-slice(bf16[8,1,128]{2,1,0:T(2,128)(2,1)S(1)} %scatter.6, bf16[8,1,1]{2,1,0:T(2,128)(2,1)S(1)} %broadcast.132, s32[]{:T(128)} %constant.94.clone.1, s32[]{:T(128)} %constant.94.clone.1, s32[]{:T(128)} %bitcast.9) | dynamic-update-slice | bytes 36 | tf_op jit(solution)/shard_map/scatter | solution.py:113
  6.4 0.9 %pad_maximum_fusion.1 = bf16[8,289,128]{2,1,0:T(8,128)(2,1)} fusion(bf16[8,1,128]{2,1,0:T(2,128)(2,1)S(1)} %scatter.9, bf16[8,32,128]{2,1,0:T(8,128)(2,1)S(1)} %bitcast.88, bf16[8,256,128]{2,1,0:T(8,128)(2,1)S(1)} %bitcast.76), kind=kLoop, calls=%fused_computation.12 | loop fusion | flops 1775616 | bytes 1183744 | tf_op jit(solution)/shard_map/concatenate | solution.py:119
  7.2 7.3 %all-to-all-start = ((bf16[8,289,128]{2,1,0:T(8,128)(2,1)}), bf16[8,289,128]{2,1,0:T(8,128)(2,1)S(1)}, u32[]{:S(2)}, u32[]{:S(2)}) async-start(bf16[8,289,128]{2,1,0:T(8,128)(2,1)} %pad_maximum_fusion.1), calls=%async_computation | async-start | bytes 1212416 | tf_op jit(solution)/shard_map/all_to_all | solution.py:120
  14.7 16.0 %all-to-all-done = bf16[8,289,128]{2,1,0:T(8,128)(2,1)S(1)} async-done(((bf16[8,289,128]{2,1,0:T(8,128)(2,1)}), bf16[8,289,128]{2,1,0:T(8,128)(2,1)S(1)}, u32[]{:S(2)}, u32[]{:S(2)}) %all-to-all-start) | async-done | bytes 591904 | tf_op jit(solution)/shard_map/all_to_all | solution.py:120
  30.9 0.4 copy.89
  31.3 0.5 copy-done.3
  31.8 0.6 gather_fusion.1
  32.4 0.2 fusion.7
  32.6 0.2 copy.82
  32.8 0.7 %gather_fusion = bf16[8,288,128]{1,2,0:T(8,128)(2,1)S(1)} fusion(bf16[8,288,128]{1,2,0:T(8,128)(2,1)S(1)} %copy.89, s32[1024]{0:T(1024)S(1)} %get-tuple-element.49), kind=kCustom, calls=%fused_computation | custom fusion | bytes 1179680 | tf_op jit(solution)/shard_map/jit(_take)/gather | solution.py:126
  33.6 0.2 broadcast_select_fusion
  33.7 0.2 pad_maximum_fusion
  33.9 1.1 %copy.83 = bf16[8,352,128]{2,1,0:T(8,128)(2,1)} copy(bf16[8,352,128]{1,2,0:T(8,128)(2,1)S(1)} %pad_maximum_fusion) | data formatting | bytes 1441792 | tf_op jit(solution)/shard_map/concatenate | solution.py:129
  35.0 3.8 %all-to-all-start.1 = ((bf16[8,352,128]{2,1,0:T(8,128)(2,1)}), bf16[8,352,128]{2,1,0:T(8,128)(2,1)S(1)}, u32[]{:S(2)}, u32[]{:S(2)}) async-start(bf16[8,352,128]{2,1,0:T(8,128)(2,1)} %copy.83), calls=%async_computation.1 | async-start | bytes 1441792 | tf_op jit(solution)/shard_map/all_to_all | solution.py:130
  38.8 0.2 broadcast_in_dim.85
  39.0 0.2 broadcast_in_dim.86
  39.2 0.3 copy.87
  39.5 0.3 multiply_cosine_fusion
  40.1 17.7 %all-to-all-done.1 = bf16[8,352,128]{2,1,0:T(8,128)(2,1)S(1)} async-done(((bf16[8,352,128]{2,1,0:T(8,128)(2,1)}), bf16[8,352,128]{2,1,0:T(8,128)(2,1)S(1)}, u32[]{:S(2)}, u32[]{:S(2)}) %all-to-all-start.1) | async-done | bytes 720928 | tf_op jit(solution)/shard_map/all_to_all | solution.py:130
  57.9 0.5 convolution_bitcast_fusion
  58.4 3.4 %psum.7 = bf16[128,64]{0,1:T(8,128)(2,1)S(1)} all-reduce(f32[128,64]{0,1:T(8,128)S(1)} %convolution_bitcast_fusion), channel_id=1, replica_groups=mesh['parts'=2,'req'=8,'mp'=2] {'mp'}, use_global_device_ids=true, to_apply=%region_1.2 | all-reduce | flops 8192 | bytes 49152 | tf_op jit(solution)/shard_map/psum | solution.py:139
  61.9 0.2 convolution_add_fusion
  62.2 0.2 slice_negate_fusion
  62.7 0.4 fusion.28
  63.2 0.2 fusion.1
  63.3 0.3 convolution_convert_fusion
  63.6 0.7 %reshape.170 = bf16[128,512]{1,0:T(8,128)(2,1)} reshape(bf16[512,128]{1,0:T(8,128)(2,1)S(1)} %convolution_convert_fusion) | data formatting | bytes 262144 | tf_op jit(solution)/shard_map/reshape | solution.py:81
  (49 shorter events, 1.5 us)
Async XLA Ops:
  0.0 57.9 %copy-start = (bf16[128,4096]{1,0:T(8,128)(2,1)S(1)}, bf16[128,4096]{1,0:T(8,128)(2,1)}, u32[]{:S(2)}) copy-start(bf16[128,4096]{1,0:T(8,128)(2,1)} %param.14) | copy-start | bytes 3145732
  4.1 0.8 %copy-start.4 = (bf16[1,1,64,512]{3,2,1,0:T(8,128)(2,1)S(1)}, bf16[1,1,64,512]{3,2,1,0:T(8,128)(2,1)}, u32[]{:S(2)}) copy-start(bf16[1,1,64,512]{3,2,1,0:T(8,128)(2,1)} %param.19) | copy-start | bytes 196612
  7.2 23.5 %all-to-all-start = ((bf16[8,289,128]{2,1,0:T(8,128)(2,1)}), bf16[8,289,128]{2,1,0:T(8,128)(2,1)S(1)}, u32[]{:S(2)}, u32[]{:S(2)}) async-start(bf16[8,289,128]{2,1,0:T(8,128)(2,1)} %pad_maximum_fusion.1), calls=%async_computation | async-start | bytes 1212416 | tf_op jit(solution)/shard_map/all_to_all | solution.py:120
  30.9 1.0 %copy-start.3 = (bf16[16,32,256]{2,1,0:T(8,128)(2,1)S(1)}, bf16[16,32,256]{2,1,0:T(8,128)(2,1)}, u32[]{:S(2)}) copy-start(bf16[16,32,256]{2,1,0:T(8,128)(2,1)} %param.17) | copy-start | bytes 786436
  35.0 4.5 %copy-start.1 = (bf16[128,256]{1,0:T(8,128)(2,1)S(1)}, bf16[128,256]{1,0:T(8,128)(2,1)}, u32[]{:S(2)}) copy-start(bf16[128,256]{1,0:T(8,128)(2,1)} %param.16) | copy-start | bytes 196612
  35.0 22.7 %all-to-all-start.1 = ((bf16[8,352,128]{2,1,0:T(8,128)(2,1)}), bf16[8,352,128]{2,1,0:T(8,128)(2,1)S(1)}, u32[]{:S(2)}, u32[]{:S(2)}) async-start(bf16[8,352,128]{2,1,0:T(8,128)(2,1)} %copy.83), calls=%async_computation.1 | async-start | bytes 1441792 | tf_op jit(solution)/shard_map/all_to_all | solution.py:130
  57.9 4.0 %copy-start.2 = (bf16[128,512]{1,0:T(8,128)(2,1)S(1)}, bf16[128,512]{1,0:T(8,128)(2,1)}, u32[]{:S(2)}) copy-start(bf16[128,512]{1,0:T(8,128)(2,1)} %param.15) | copy-start | bytes 393220
where the time goes:
time: 64.9 us; the launch traced here: 64.4 us
  waiting for transfers between devices  33.7 us (52%)
  starting transfers between devices  11 us (17%)
  local copies, waits for them, and re-layouts  9.87 us (15%)
  blocking collectives  3.41 us (5%)
  other arithmetic  3.15 us (5%)
  between operations  1.79 us (3%)
  matrix products  1.43 us (2%)
    all_to_all x1, waiting for transfers between devices, on_device(): lax.all_to_all(stage_two, 'req', split_axis=0, concat_axis=0, tiled=True)  17.7 us
    all_to_all x1, waiting for transfers between devices, on_device(): lax.all_to_all(stage_one, 'req', split_axis=0, concat_axis=0, tiled=True)  16 us
    all_to_all x1, starting transfers between devices, on_device(): lax.all_to_all(stage_one, 'req', split_axis=0, concat_axis=0, tiled=True)  7.25 us
    all_to_all x1, starting transfers between devices, on_device(): lax.all_to_all(stage_two, 'req', split_axis=0, concat_axis=0, tiled=True)  3.77 us
    psum x1, blocking collectives, on_device(): rank_reduce = lax.psum(partial_value, 'mp').astype(jnp.bfloat16)  3.41 us
    unnamed x14, local copies, waits for them, and re-layouts  2.72 us
    scatter x1, local copies, waits for them, and re-layouts, on_device(): asks = asks.at[:, 0, 1].set(request_adapter[0].astype(jnp.float32))  1.33 us
  transfers between devices with their start and end apart: 2, of which 2 were waited for; matrix products, arithmetic and copies ran while one was open for 2% of the time, Pallas kernels for 0%

commit v1 on v0

--- a/solution.py
+++ b/solution.py
@@ -7,6 +7,28 @@
 ROPE_BASE = 500000.0
 LANES = 128
 TILE_ROWS = 16
+
+
+def in_blocks(x, dim, size):
+    before, after = (x.shape[:dim], x.shape[dim + 1 :])
+    return jnp.moveaxis(x.reshape(*before, size, -1, *after), dim, 0)
+
+
+def laid_out(blocks, dim):
+    lengths = list(blocks.shape[1:])
+    lengths[dim] *= blocks.shape[0]
+    return jnp.moveaxis(blocks, 0, dim).reshape(lengths)
+
+
+def pairwise_exchange(shard, axis, split_dim, concat_dim):
+    devices, index = (lax.axis_size(axis), lax.axis_index(axis))
+    tiles = in_blocks(shard, split_dim, devices)
+    outs = [tiles[index]]
+    for step in range(1, devices):
+        sent = tiles[index ^ step]
+        outs.append(lax.ppermute(sent, axis, [(i, i ^ step) for i in range(devices)]))
+    tiles = jnp.stack(outs)[index ^ jnp.arange(devices)]
+    return laid_out(tiles, concat_dim)
 
 
 def rotate(vectors, positions):
@@ -117,7 +139,7 @@
         parts_out.append(to_pieces(adapter_up_weight[a, 0], groups))
     parts_out.append(asks.astype(jnp.bfloat16))
     stage_one = jnp.concatenate(parts_out, axis=1)
-    stage_one = lax.all_to_all(stage_one, "req", split_axis=0, concat_axis=0, tiled=True)
+    stage_one = pairwise_exchange(stage_one, "req", 0, 0)
     share_rows = down_rows + up_rows
     shares = stage_one[:, : held * share_rows].reshape(groups * held, share_rows, LANES)
     their_asks = stage_one[:, held * share_rows, :2].astype(jnp.int32)

time: 64.9 us -> 62.5 us (0.963)
  waiting for transfers between devices: 33.7 us -> 24.5 us
  starting transfers between devices: 11 us -> 18 us
  other arithmetic: 3.15 us -> 2.33 us
    all_to_all x1 -> x0, waiting for transfers between devices: 16 us -> none  [on_device(): lax.all_to_all(stage_one, 'req', split_axis=0, concat_axis=0, tiled=True)]
    ppermute x0 -> x7, starting transfers between devices: none -> 12.6 us  [pairwise_exchange(): lax.ppermute(sent, axis, [(i, i ^ step) for i in range(devices)])]
    all_to_all x1 -> x0, starting transfers between devices: 7.25 us -> none  [on_device(): lax.all_to_all(stage_one, 'req', split_axis=0, concat_axis=0, tiled=True)]
    ppermute x0 -> x7, waiting for transfers between devices: none -> 7.04 us  [pairwise_exchange(): lax.ppermute(sent, axis, [(i, i ^ step) for i in range(devices)])]
    all_to_all x1, starting transfers between devices: 3.77 us -> 5.41 us  [on_device(): lax.all_to_all(stage_two, 'req', split_axis=0, concat_axis=0, tiled=True)]
    concatenate x1, other arithmetic: 0.87 us -> 0.04 us  [on_device(): stage_one = jnp.concatenate(parts_out, axis=1)]
    gather x0 -> x1, local copies, waits for them, and re-layouts: none -> 0.67 us  [pairwise_exchange(): tiles = jnp.stack(outs)[index ^ jnp.arange(devices)]]
    unnamed x14 -> x20, local copies, waits for them, and re-layouts: 2.72 us -> 2.32 us
  transfers between devices with their start and end apart: 2 -> 8, of which waited for: 2 -> 3; matrix products, arithmetic and copies ran while one was open for 2% -> 2% of each run, Pallas kernels for 0% -> 0%
where the time goes in v1:
time: 62.5 us; the launch traced here: 62.1 us
  waiting for transfers between devices  24.5 us (39%)
  starting transfers between devices  18 us (29%)
  local copies, waits for them, and re-layouts  10.5 us (17%)
  blocking collectives  3.41 us (5%)
  other arithmetic  2.33 us (4%)
  between operations  1.94 us (3%)
  matrix products  1.43 us (2%)
    all_to_all x1, waiting for transfers between devices, on_device(): lax.all_to_all(stage_two, 'req', split_axis=0, concat_axis=0, tiled=True)  17.5 us
    ppermute x7, starting transfers between devices, pairwise_exchange(): lax.ppermute(sent, axis, [(i, i ^ step) for i in range(devices)])  12.6 us
    ppermute x7, waiting for transfers between devices, pairwise_exchange(): lax.ppermute(sent, axis, [(i, i ^ step) for i in range(devices)])  7.04 us
    all_to_all x1, starting transfers between devices, on_device(): lax.all_to_all(stage_two, 'req', split_axis=0, concat_axis=0, tiled=True)  5.41 us
    psum x1, blocking collectives, on_device(): rank_reduce = lax.psum(partial_value, 'mp').astype(jnp.bfloat16)  3.41 us
    unnamed x20, local copies, waits for them, and re-layouts  2.32 us
    scatter x1, local copies, waits for them, and re-layouts, on_device(): asks = asks.at[:, 0, 1].set(request_adapter[0].astype(jnp.float32))  1.27 us
  transfers between devices with their start and end apart: 8, of which 3 were waited for; matrix products, arithmetic and copies ran while one was open for 2% of the time, Pallas kernels for 0%

profile of v1, /device:TPU:0, one launch (start us, length us, event | category | flops | bytes accessed | tf_op | source)
XLA Modules:
  0.0 62.1 jit_solution(3182965527065117216)
XLA Ops:
  0.8 0.8 %select_reduce_fusion = s32[8]{0:T(128)S(1)} fusion(s32[8]{0:T(128)} %bitcast.124, s32[8]{0:T(128)} %bitcast.125, pred[8]{0:T(512)(128)(4,1)S(1)} %iota_compare_fusion.2), kind=kLoop, calls=%fused_computation.58 | loop fusion | flops 248 | bytes 104 | tf_op jit(solution)/shard_map/reduce_max | solution.py:132
  2.3 0.6 slice.88
  2.9 1.1 %copy.123 = bf16[8,8,32,128]{3,2,1,0:T(8,128)(2,1)S(1)} copy(bf16[8,8,32,128]{3,1,2,0:T(8,128)(2,1)} %bitcast.116) | data formatting | bytes 1048576
  4.1 0.2 copy.104
  4.4 0.6 copy-done.4
  5.0 1.3 %scatter.9 = bf16[8,1,128]{2,1,0:T(2,128)(2,1)S(1)} dynamic-update-slice(bf16[8,1,128]{2,1,0:T(2,128)(2,1)S(1)} %scatter.6, bf16[8,1,1]{2,1,0:T(2,128)(2,1)S(1)} %broadcast.156, s32[]{:T(128)} %constant.108.clone.1, s32[]{:T(128)} %constant.108.clone.1, s32[]{:T(128)} %bitcast.9) | dynamic-update-slice | bytes 36 | tf_op jit(solution)/shard_map/scatter | solution.py:135
  6.4 3.0 %collective-permute-start = (bf16[1,289,128]{2,1,0:T(8,128)(2,1)S(1)}, bf16[1,289,128]{2,1,0:T(8,128)(2,1)S(1)}, u32[]{:S(2)}, u32[]{:S(2)}) collective-permute-start(bf16[1,289,128]{2,1,0:T(8,128)(2,1)S(1)} %get-tuple-element.35), channel_id=1, source_target_pairs={{0,2},{2,0},{4,6},{6,4},{8,10},{10,8},{12,14},{14,12},{1,3},{3,1},... | collective-permute-start | bytes 221960 | tf_op jit(solution)/shard_map/ppermute | solution.py:29
  9.4 1.6 %collective-permute-start.1 = (bf16[1,289,128]{2,1,0:T(8,128)(2,1)S(1)}, bf16[1,289,128]{2,1,0:T(8,128)(2,1)S(1)}, u32[]{:S(2)}, u32[]{:S(2)}) collective-permute-start(bf16[1,289,128]{2,1,0:T(8,128)(2,1)S(1)} %get-tuple-element.34), channel_id=1, source_target_pairs={{0,4},{2,6},{4,0},{6,2},{8,12},{10,14},{12,8},{14,10},{1,5},{3,7},... | collective-permute-start | bytes 221960 | tf_op jit(solution)/shard_map/ppermute | solution.py:29
  11.0 3.0 %collective-permute-start.3 = (bf16[1,289,128]{2,1,0:T(8,128)(2,1)S(1)}, bf16[1,289,128]{2,1,0:T(8,128)(2,1)S(1)}, u32[]{:S(2)}, u32[]{:S(2)}) collective-permute-start(bf16[1,289,128]{2,1,0:T(8,128)(2,1)S(1)} %get-tuple-element.32), channel_id=1, source_target_pairs={{0,8},{2,10},{4,12},{6,14},{8,0},{10,2},{12,4},{14,6},{1,9},{3,11}... | collective-permute-start | bytes 221960 | tf_op jit(solution)/shard_map/ppermute | solution.py:29
  14.0 1.3 %collective-permute-start.4 = (bf16[1,289,128]{2,1,0:T(8,128)(2,1)S(1)}, bf16[1,289,128]{2,1,0:T(8,128)(2,1)S(1)}, u32[]{:S(2)}, u32[]{:S(2)}) collective-permute-start(bf16[1,289,128]{2,1,0:T(8,128)(2,1)S(1)} %get-tuple-element.31), channel_id=1, source_target_pairs={{0,10},{2,8},{4,14},{6,12},{8,2},{10,0},{12,6},{14,4},{1,11},{3,9}... | collective-permute-start | bytes 221960 | tf_op jit(solution)/shard_map/ppermute | solution.py:29
  15.5 3.7 %collective-permute-start.5 = (bf16[1,289,128]{2,1,0:T(8,128)(2,1)S(1)}, bf16[1,289,128]{2,1,0:T(8,128)(2,1)S(1)}, u32[]{:S(2)}, u32[]{:S(2)}) collective-permute-start(bf16[1,289,128]{2,1,0:T(8,128)(2,1)S(1)} %get-tuple-element.30), channel_id=1, source_target_pairs={{0,12},{2,14},{4,8},{6,10},{8,4},{10,6},{12,0},{14,2},{1,13},{3,15... | collective-permute-start | bytes 221960 | tf_op jit(solution)/shard_map/ppermute | solution.py:29
  19.4 6.1 %collective-permute-done.4 = bf16[1,289,128]{2,1,0:T(8,128)(2,1)S(1)} collective-permute-done((bf16[1,289,128]{2,1,0:T(8,128)(2,1)S(1)}, bf16[1,289,128]{2,1,0:T(8,128)(2,1)S(1)}, u32[]{:S(2)}, u32[]{:S(2)}) %collective-permute-start.4) | collective-permute-done | bytes 74016 | tf_op jit(solution)/shard_map/ppermute | solution.py:29
  25.6 0.9 %collective-permute-done.6 = bf16[1,289,128]{2,1,0:T(8,128)(2,1)S(1)} collective-permute-done((bf16[1,289,128]{2,1,0:T(8,128)(2,1)S(1)}, bf16[1,289,128]{2,1,0:T(8,128)(2,1)S(1)}, u32[]{:S(2)}, u32[]{:S(2)}) %collective-permute-start.6) | collective-permute-done | bytes 74016 | tf_op jit(solution)/shard_map/ppermute | solution.py:29
  26.5 0.7 %gather_fusion = bf16[8,289,128]{2,1,0:T(8,128)(2,1)S(1)} fusion(bf16[8,289,128]{2,1,0:T(8,128)(2,1)S(1)} %bitcast.114, s32[1024]{0:T(1024)S(1)} %pad_clamp_fusion.2), kind=kCustom, calls=%fused_computation | custom fusion | bytes 1183776 | tf_op jit(solution)/shard_map/gather | solution.py:30
  27.4 0.4 copy.114
  27.7 0.4 copy-done.3
  28.1 0.6 gather_fusion.2
  28.7 0.2 fusion.7
  29.1 0.7 %gather_fusion.1 = bf16[8,288,128]{1,2,0:T(8,128)(2,1)S(1)} fusion(bf16[8,288,128]{1,2,0:T(8,128)(2,1)S(1)} %copy.114, s32[1024]{0:T(1024)S(1)} %get-tuple-element.56), kind=kCustom, calls=%fused_computation.1 | custom fusion | bytes 1179680 | tf_op jit(solution)/shard_map/jit(_take)/gather | solution.py:148
  30.2 1.1 %copy.117 = bf16[8,352,128]{2,1,0:T(8,128)(2,1)} copy(bf16[8,352,128]{1,2,0:T(8,128)(2,1)S(1)} %pad_maximum_fusion) | data formatting | bytes 1441792 | tf_op jit(solution)/shard_map/concatenate | solution.py:151
  31.3 5.4 %all-to-all-start = ((bf16[8,352,128]{2,1,0:T(8,128)(2,1)}), bf16[8,352,128]{2,1,0:T(8,128)(2,1)S(1)}, u32[]{:S(2)}, u32[]{:S(2)}) async-start(bf16[8,352,128]{2,1,0:T(8,128)(2,1)} %copy.117), calls=%async_computation | async-start | bytes 1441792 | tf_op jit(solution)/shard_map/all_to_all | solution.py:152
  36.8 0.2 broadcast_in_dim.86
  37.1 0.3 copy.121
  37.5 0.3 multiply_cosine_fusion
  38.0 17.5 %all-to-all-done = bf16[8,352,128]{2,1,0:T(8,128)(2,1)S(1)} async-done(((bf16[8,352,128]{2,1,0:T(8,128)(2,1)}), bf16[8,352,128]{2,1,0:T(8,128)(2,1)S(1)}, u32[]{:S(2)}, u32[]{:S(2)}) %all-to-all-start) | async-done | bytes 720928 | tf_op jit(solution)/shard_map/all_to_all | solution.py:152
  55.6 0.5 convolution_bitcast_fusion
  56.1 3.4 %psum.7 = bf16[128,64]{0,1:T(8,128)(2,1)S(1)} all-reduce(f32[128,64]{0,1:T(8,128)S(1)} %convolution_bitcast_fusion), channel_id=1, replica_groups=mesh['parts'=2,'req'=8,'mp'=2] {'mp'}, use_global_device_ids=true, to_apply=%region_1.2 | all-reduce | flops 8192 | bytes 49152 | tf_op jit(solution)/shard_map/psum | solution.py:161
  59.6 0.2 convolution_add_fusion
  59.9 0.2 slice_negate_fusion
  60.4 0.4 fusion.29
  61.0 0.3 convolution_convert_fusion
  61.3 0.7 %reshape.206 = bf16[128,512]{1,0:T(8,128)(2,1)} reshape(bf16[512,128]{1,0:T(8,128)(2,1)S(1)} %convolution_convert_fusion) | data formatting | bytes 262144 | tf_op jit(solution)/shard_map/reshape | solution.py:103
  (73 shorter events, 2.6 us)
Async XLA Ops:
  0.0 55.6 %copy-start = (bf16[128,4096]{1,0:T(8,128)(2,1)S(1)}, bf16[128,4096]{1,0:T(8,128)(2,1)}, u32[]{:S(2)}) copy-start(bf16[128,4096]{1,0:T(8,128)(2,1)} %param.14) | copy-start | bytes 3145732
  4.1 0.8 %copy-start.4 = (bf16[1,1,64,512]{3,2,1,0:T(8,128)(2,1)S(1)}, bf16[1,1,64,512]{3,2,1,0:T(8,128)(2,1)}, u32[]{:S(2)}) copy-start(bf16[1,1,64,512]{3,2,1,0:T(8,128)(2,1)} %param.19) | copy-start | bytes 196612
  6.4 9.1 %collective-permute-start = (bf16[1,289,128]{2,1,0:T(8,128)(2,1)S(1)}, bf16[1,289,128]{2,1,0:T(8,128)(2,1)S(1)}, u32[]{:S(2)}, u32[]{:S(2)}) collective-permute-start(bf16[1,289,128]{2,1,0:T(8,128)(2,1)S(1)} %get-tuple-element.35), channel_id=1, source_target_pairs={{0,2},{2,0},{4,6},{6,4},{8,10},{10,8},{12,14},{14,12},{1,3},{3,1},... | collective-permute-start | bytes 221960 | tf_op jit(solution)/shard_map/ppermute | solution.py:29
  9.4 9.8 %collective-permute-start.1 = (bf16[1,289,128]{2,1,0:T(8,128)(2,1)S(1)}, bf16[1,289,128]{2,1,0:T(8,128)(2,1)S(1)}, u32[]{:S(2)}, u32[]{:S(2)}) collective-permute-start(bf16[1,289,128]{2,1,0:T(8,128)(2,1)S(1)} %get-tuple-element.34), channel_id=1, source_target_pairs={{0,4},{2,6},{4,0},{6,2},{8,12},{10,14},{12,8},{14,10},{1,5},{3,7},... | collective-permute-start | bytes 221960 | tf_op jit(solution)/shard_map/ppermute | solution.py:29
  11.0 8.3 %collective-permute-start.2 = (bf16[1,289,128]{2,1,0:T(8,128)(2,1)S(1)}, bf16[1,289,128]{2,1,0:T(8,128)(2,1)S(1)}, u32[]{:S(2)}, u32[]{:S(2)}) collective-permute-start(bf16[1,289,128]{2,1,0:T(8,128)(2,1)S(1)} %get-tuple-element.33), channel_id=1, source_target_pairs={{0,6},{2,4},{4,2},{6,0},{8,14},{10,12},{12,10},{14,8},{1,7},{3,5},... | collective-permute-start | bytes 221960 | tf_op jit(solution)/shard_map/ppermute | solution.py:29
  11.0 8.3 %collective-permute-start.3 = (bf16[1,289,128]{2,1,0:T(8,128)(2,1)S(1)}, bf16[1,289,128]{2,1,0:T(8,128)(2,1)S(1)}, u32[]{:S(2)}, u32[]{:S(2)}) collective-permute-start(bf16[1,289,128]{2,1,0:T(8,128)(2,1)S(1)} %get-tuple-element.32), channel_id=1, source_target_pairs={{0,8},{2,10},{4,12},{6,14},{8,0},{10,2},{12,4},{14,6},{1,9},{3,11}... | collective-permute-start | bytes 221960 | tf_op jit(solution)/shard_map/ppermute | solution.py:29
  14.0 11.5 %collective-permute-start.4 = (bf16[1,289,128]{2,1,0:T(8,128)(2,1)S(1)}, bf16[1,289,128]{2,1,0:T(8,128)(2,1)S(1)}, u32[]{:S(2)}, u32[]{:S(2)}) collective-permute-start(bf16[1,289,128]{2,1,0:T(8,128)(2,1)S(1)} %get-tuple-element.31), channel_id=1, source_target_pairs={{0,10},{2,8},{4,14},{6,12},{8,2},{10,0},{12,6},{14,4},{1,11},{3,9}... | collective-permute-start | bytes 221960 | tf_op jit(solution)/shard_map/ppermute | solution.py:29
  15.5 10.0 %collective-permute-start.5 = (bf16[1,289,128]{2,1,0:T(8,128)(2,1)S(1)}, bf16[1,289,128]{2,1,0:T(8,128)(2,1)S(1)}, u32[]{:S(2)}, u32[]{:S(2)}) collective-permute-start(bf16[1,289,128]{2,1,0:T(8,128)(2,1)S(1)} %get-tuple-element.30), channel_id=1, source_target_pairs={{0,12},{2,14},{4,8},{6,10},{8,4},{10,6},{12,0},{14,2},{1,13},{3,15... | collective-permute-start | bytes 221960 | tf_op jit(solution)/shard_map/ppermute | solution.py:29
  19.2 7.2 %collective-permute-start.6 = (bf16[1,289,128]{2,1,0:T(8,128)(2,1)S(1)}, bf16[1,289,128]{2,1,0:T(8,128)(2,1)S(1)}, u32[]{:S(2)}, u32[]{:S(2)}) collective-permute-start(bf16[1,289,128]{2,1,0:T(8,128)(2,1)S(1)} %get-tuple-element.29), channel_id=1, source_target_pairs={{0,14},{2,12},{4,10},{6,8},{8,6},{10,4},{12,2},{14,0},{1,15},{3,13... | collective-permute-start | bytes 221960 | tf_op jit(solution)/shard_map/ppermute | solution.py:29
  27.2 1.0 %copy-start.3 = (bf16[16,32,256]{2,1,0:T(8,128)(2,1)S(1)}, bf16[16,32,256]{2,1,0:T(8,128)(2,1)}, u32[]{:S(2)}) copy-start(bf16[16,32,256]{2,1,0:T(8,128)(2,1)} %param.17) | copy-start | bytes 786436
  31.3 6.1 %copy-start.1 = (bf16[128,256]{1,0:T(8,128)(2,1)S(1)}, bf16[128,256]{1,0:T(8,128)(2,1)}, u32[]{:S(2)}) copy-start(bf16[128,256]{1,0:T(8,128)(2,1)} %param.16) | copy-start | bytes 196612
  31.3 24.1 %all-to-all-start = ((bf16[8,352,128]{2,1,0:T(8,128)(2,1)}), bf16[8,352,128]{2,1,0:T(8,128)(2,1)S(1)}, u32[]{:S(2)}, u32[]{:S(2)}) async-start(bf16[8,352,128]{2,1,0:T(8,128)(2,1)} %copy.117), calls=%async_computation | async-start | bytes 1441792 | tf_op jit(solution)/shard_map/all_to_all | solution.py:152
  55.6 4.0 %copy-start.2 = (bf16[128,512]{1,0:T(8,128)(2,1)S(1)}, bf16[128,512]{1,0:T(8,128)(2,1)}, u32[]{:S(2)}) copy-start(bf16[128,512]{1,0:T(8,128)(2,1)} %param.15) | copy-start | bytes 393220
